TPU v7x, 512 devices: a whole 4x8x8 slice. The times are simulated.
512 devices in a mesh: exp: 128 (over y, z, core), hid: 4 (over x).
Axes of the slice: x: 4, y: 8, z: 8, core: 2. Of those that a mesh axis runs over, the one named last changes fastest.
Arguments:
- tokens: bfloat16 [4096, 4096], P('exp', 'hid'), may hold values from -6 to 6
- expert_ids: int32 [4096, 8], P('exp'), may hold values from 0 to 127, all different within a row; in each aligned block of 16 rows (0 to 15, 16 to 31, ...) at most 2 rows name the same one
- combine: float32 [4096, 8], P('exp'), may hold values from 0.05 to 0.4
- sign_bits: int32 [128, 768], P('exp'), may hold values from 0 to 1
- w_gate: bfloat16 [128, 768, 4096], P('exp', 'hid'), may hold values from -0.09375 to 0.09375
- w_up: bfloat16 [128, 768, 4096], P('exp', 'hid'), may hold values from -0.09375 to 0.09375
- w_down: bfloat16 [128, 768, 4096], P('exp', 'hid'), may hold values from -0.21875 to 0.21875
Outputs:
- next_input: bfloat16 [4096, 4096], P('exp', 'hid')
- hessian: bfloat16 [128, 768, 768], P('exp', 'hid')
Inputs may be any that keep to these rules, and one draw needn't show every extreme that they name: `expert_ids`: each row names 8 different experts. Within each aligned block of 16 rows (one micro-batch of one index of exp) no expert is named by more than 2 rows, a bound that some block reaches. `sign_bits`: 0 stands for the sign -1, 1 for +1.
All inputs are finite; a program needn't handle non-finite values.
Results may differ from a plain program's by a relative error of at most 0.0065.
Values may be sent and summed in bfloat16 or wider, within the bound.
No kernel may reach another device: no remote copies, remote signals or barrier semaphores. Data moves between devices by JAX's collectives and lax.ppermute only.
A program may use at most 64 MiB of HBM per device.

v0:
```python
import jax
import jax.numpy as jnp
import numpy as np
from jax import lax
from jax.sharding import PartitionSpec as P


def paley_twelve():
    residues = set((number * number % 11 for number in range(1, 11)))
    legendre = [0] + [1 if number in residues else -1 for number in range(1, 11)]
    hadamard = np.zeros((12, 12))
    hadamard[0, 1:] = 1.0
    hadamard[1:, 0] = -1.0
    for row_index in range(11):
        for col_index in range(11):
            hadamard[row_index + 1, col_index + 1] = legendre[(col_index - row_index) % 11]
    return hadamard + np.eye(12)


def sylvester(order_size):
    positions = jnp.arange(order_size, dtype=jnp.int32)
    common = positions[:, None] & positions[None, :]
    parity = jnp.zeros_like(common)
    for bit_pos in range(order_size.bit_length()):
        parity = parity + (common >> bit_pos & 1)
    return (1 - 2 * (parity % 2)).astype(jnp.float32)


def rotate(hidden, sign_rows, paley_table, sylvester_table):
    values = hidden.astype(jnp.float32) * jnp.expand_dims(sign_rows, -2)
    blocks = values.reshape(values.shape[:-1] + (12, sylvester_table.shape[0]))
    turned = jnp.einsum(
        "...ab,ca,db->...cd", blocks, paley_table, sylvester_table, precision=lax.Precision.HIGHEST
    )
    return turned.reshape(values.shape)


def rank_of_pick(ids_block, experts):
    flat_ids = ids_block.reshape(-1)
    onehot = (flat_ids[:, None] == jnp.arange(experts, dtype=jnp.int32)[None, :]).astype(jnp.int32)
    before = jnp.cumsum(onehot, axis=0) - onehot
    return jnp.sum(before * onehot, axis=1).reshape(ids_block.shape)


def local(tokens, expert_ids, combine, sign_bits, w_gate, w_up, w_down):
    n_exp = lax.axis_size("exp")
    n_hid = lax.axis_size("hid")
    hid_index = lax.axis_index("hid")
    local_experts = w_gate.shape[0]
    experts = local_experts * n_exp
    tok_rows = tokens.shape[0]
    half_rows = tok_rows // 2
    top_count = expert_ids.shape[1]
    capacity = min(half_rows, max(2, 2 * half_rows * top_count // experts))
    hidden_units = sign_bits.shape[1]
    share_rows = hidden_units // n_hid
    slot_count = n_exp * capacity
    paley_table = jnp.asarray(paley_twelve(), jnp.float32)
    sylvester_table = sylvester(hidden_units // 12)
    sign_rows = (2 * sign_bits - 1).astype(jnp.float32)
    gram_scale = experts / (tok_rows * n_exp * top_count * hidden_units)
    down_cols = lax.all_to_all(w_down, "hid", split_axis=2, concat_axis=1, tiled=True)
    gram_total = jnp.zeros((local_experts, share_rows, hidden_units), jnp.float32)
    results = []
    for batch_index in range(2):
        first_row = batch_index * half_rows
        ids_block = expert_ids[first_row : first_row + half_rows]
        picks_rank = rank_of_pick(ids_block, experts)
        target = ids_block * capacity + picks_rank
        selector = jnp.any(
            target[None, :, :] == jnp.arange(experts * capacity, dtype=jnp.int32)[:, None, None],
            axis=2,
        ).astype(jnp.bfloat16)
        sending = jnp.dot(
            selector, tokens[first_row : first_row + half_rows], preferred_element_type=jnp.float32
        ).astype(jnp.bfloat16)
        arrived = lax.all_to_all(sending, "exp", split_axis=0, concat_axis=0, tiled=True)
        arrived = lax.all_gather(arrived, "hid", axis=1, tiled=True)
        row_width = arrived.shape[1]
        expert_in = arrived.reshape(n_exp, local_experts, capacity, row_width).transpose(1, 0, 2, 3)
        expert_in = expert_in.reshape(local_experts, slot_count, row_width)
        gate_act = jnp.einsum("esd,efd->esf", expert_in, w_gate, preferred_element_type=jnp.float32)
        up_act = jnp.einsum("esd,efd->esf", expert_in, w_up, preferred_element_type=jnp.float32)
        hidden = (jax.nn.silu(gate_act) * up_act).astype(jnp.bfloat16)
        full_hidden = lax.all_gather(hidden, "hid", axis=2, tiled=True)
        summed = jnp.einsum(
            "esf,efd->esd", full_hidden, down_cols, preferred_element_type=jnp.float32
        ).astype(jnp.bfloat16)
        outgoing = summed.reshape(local_experts, n_exp, capacity, -1).transpose(1, 0, 2, 3)
        outgoing = outgoing.reshape(n_exp * local_experts * capacity, -1)
        back_rows = lax.all_to_all(outgoing, "exp", split_axis=0, concat_axis=0, tiled=True)
        picked = back_rows[target]
        weights = combine[first_row : first_row + half_rows]
        mixed_rows = tokens[first_row : first_row + half_rows].astype(jnp.float32) + jnp.sum(
            weights[:, :, None] * picked.astype(jnp.float32), axis=1
        )
        results.append(mixed_rows.astype(jnp.bfloat16))
        rotated = rotate(full_hidden, sign_rows, paley_table, sylvester_table)
        own_rotated = lax.dynamic_slice_in_dim(rotated, hid_index * share_rows, share_rows, 2)
        gram_total = gram_total + jnp.einsum(
            "esi,esj->eij", own_rotated, rotated, precision=lax.Precision.HIGHEST
        )
    hessian = (gram_total * gram_scale).astype(jnp.bfloat16)
    return (jnp.concatenate(results, axis=0), hessian)


def solution(mesh):
    placed = (
        P("exp", "hid"),
        P("exp", None),
        P("exp", None),
        P("exp", None),
        P("exp", "hid", None),
        P("exp", "hid", None),
        P("exp", "hid", None),
    )
    return jax.shard_map(
        local,
        mesh=mesh,
        in_specs=placed,
        out_specs=(P("exp", "hid"), P("exp", "hid", None)),
        check_vma=False,
    )
```

profile of v0, /device:TPU:1, one launch (start us, length us, event | category | flops | bytes accessed | tf_op | source)
XLA Modules:
  0.0 254.6 jit_solution(8127304555894847153)
XLA Ops:
  7.2 0.9 fusion.82
  8.1 0.1 copy.50
  8.2 0.1 eq.65
  8.3 0.1 fusion.40
  8.4 0.2 reduce_window_sum.18
  8.5 0.2 select_reduce_fusion
  8.7 0.1 reshape.129
  8.8 0.1 fusion.39
  9.0 1.1 convolution_convert_fusion.1
  10.1 0.2 all_to_all.52
  10.3 37.8 %all_to_all.63 = bf16[128,2,1024]{2,1,0:T(2,128)(2,1)S(1)} all-to-all(bf16[128,2,1024]{2,1,0:T(2,128)(2,1)S(1)} %all_to_all.52), channel_id=1, replica_groups=mesh['exp'=128,'hid'=4] {'exp'}, dimensions={0} | all-to-all | bytes 1048576 | tf_op jit(solution)/shard_map/all_to_all | solution.py:77
  48.0 1.0 all_to_all.54
  49.2 0.1 eq.58
  49.3 0.1 fusion.41
  49.4 0.2 reduce_window_sum.17
  49.5 0.2 select_reduce_fusion.1
  49.7 0.1 reshape.124
  49.8 0.1 fusion.38
  50.0 0.3 convolution_convert_fusion.3
  50.3 0.2 all_to_all.43
  50.5 26.2 %all_to_all.64 = bf16[128,2,1024]{2,1,0:T(2,128)(2,1)S(1)} all-to-all(bf16[128,2,1024]{2,1,0:T(2,128)(2,1)S(1)} %all_to_all.43), channel_id=1, replica_groups=mesh['exp'=128,'hid'=4] {'exp'}, dimensions={0} | all-to-all | bytes 1048576 | tf_op jit(solution)/shard_map/all_to_all | solution.py:77
  76.7 1.0 all_to_all.45
  77.7 9.9 %copy.40 = bf16[1,192,4096]{1,0,2:T(2,128)(2,1)} copy(bf16[1,192,4096]{2,1,0:T(8,128)(2,1)} %param.14) | data formatting | bytes 3145728 | tf_op args[6]
  87.6 0.5 broadcast.82
  88.1 25.0 %reduce.2 = bf16[4096,192]{1,0:T(8,128)(2,1)} reduce(bf16[4096,1,192]{2,1,0:T(2,128)(2,1)} %bitcast.77, bf16[]{:T(256)} %broadcast.82), dimensions={1}, to_apply=%bitcast.61.reduce_sub_computation | reduce | bytes 3145730
  113.1 5.0 %reshape.170 = bf16[4,2,98304]{2,1,0:T(2,128)(2,1)} reshape(bf16[4096,192]{1,0:T(8,128)(2,1)} %reduce.2) | data formatting | bytes 3145728
  118.1 4.1 %all-to-all-start.1 = ((bf16[4,2,98304]{2,1,0:T(2,128)(2,1)}), bf16[4,2,98304]{2,1,0:T(2,128)(2,1)S(1)}, u32[]{:S(2)}, u32[]{:S(2)}) async-start(bf16[4,2,98304]{2,1,0:T(2,128)(2,1)} %reshape.170), calls=%async_computation.1 | async-start | bytes 3145728 | tf_op jit(solution)/shard_map/all_to_all | solution.py:62
  122.3 0.1 reshape.149
  122.4 0.7 copy.43
  123.1 0.1 reshape.141
  123.2 0.7 copy.38
  123.9 0.6 convert_reduce_fusion
  124.5 16.4 %all-to-all-done.1 = bf16[4,2,98304]{2,1,0:T(2,128)(2,1)S(1)} async-done(((bf16[4,2,98304]{2,1,0:T(2,128)(2,1)}), bf16[4,2,98304]{2,1,0:T(2,128)(2,1)S(1)}, u32[]{:S(2)}, u32[]{:S(2)}) %all-to-all-start.1) | async-done | bytes 1572896 | tf_op jit(solution)/shard_map/all_to_all | solution.py:62
  140.9 4.1 %reshape.171 = bf16[4096,1,192]{2,1,0:T(2,128)(2,1)} reshape(bf16[4,2,98304]{2,1,0:T(2,128)(2,1)S(1)} %all-to-all-done.1) | data formatting | bytes 3145728
  145.0 9.6 %copy.41 = bf16[1,192,4096]{2,1,0:T(8,128)(2,1)} copy(bf16[1,192,4096]{1,0,2:T(2,128)(2,1)} %bitcast.78) | data formatting | bytes 3145728 | tf_op jit(solution)/shard_map/all_to_all | solution.py:62
  154.6 2.9 %all_to_all.47 = bf16[1,192,4,1024]{3,2,1,0:T(4,128)(2,1)S(1)} reshape(bf16[1,192,4096]{2,1,0:T(8,128)(2,1)} %copy.41) | data formatting | bytes 3145728 | tf_op jit(solution)/shard_map/all_to_all | solution.py:62
  157.5 1.6 copy.42
  159.1 2.6 %fusion.4 = f32[256,192]{0,1:T(8,128)S(1)} fusion(bf16[256,4096]{1,0:T(8,128)(2,1)} %all-gather.7.cloned.1.call-done, bf16[1,192,4096]{2,1,0:T(8,128)(2,1)S(1)} %copy-done), kind=kOutput, calls=%fused_computation.6 | convolution fusion | flops 402653184 | bytes 3866624 | tf_op jit(solution)/shard_map/esd,efd->esf/dot_general | solution.py:82
  161.8 0.9 fusion.17
  162.7 9.6 %all-gather.1 = bf16[256,768]{0,1:T(8,128)(2,1)S(1)} all-gather(bf16[256,192]{0,1:T(8,128)(2,1)S(1)} %fusion.17), channel_id=3, replica_groups=mesh['exp'=128,'hid'=4] {'hid'}, dimensions={1}, use_global_device_ids=true | all-gather | bytes 491520 | tf_op jit(solution)/shard_map/all_gather | solution.py:85
  172.3 1.4 convolution_convert_fusion
  173.7 2.0 all_to_all.55
  175.7 12.7 %all-to-all-start.4 = ((bf16[128,2,1024]{2,1,0:T(2,128)(2,1)}), bf16[128,2,1024]{2,1,0:T(2,128)(2,1)}, u32[]{:S(2)}, u32[]{:S(2)}) async-start(bf16[128,2,1024]{2,1,0:T(2,128)(2,1)} %all_to_all.55), calls=%async_computation.4 | async-start | bytes 1048576 | tf_op jit(solution)/shard_map/all_to_all | solution.py:91
  188.5 2.6 %fusion.6 = f32[256,192]{0,1:T(8,128)S(1)} fusion(bf16[256,4096]{1,0:T(8,128)(2,1)} %all-gather.5.cloned.1.call-done, bf16[1,192,4096]{2,1,0:T(8,128)(2,1)S(1)} %copy-done), kind=kOutput, calls=%fused_computation.8 | convolution fusion | flops 402653184 | bytes 3866624 | tf_op jit(solution)/shard_map/esd,efd->esf/dot_general | solution.py:82
  191.1 0.8 fusion.20
  192.0 10.8 %all-gather = bf16[256,768]{0,1:T(8,128)(2,1)S(1)} all-gather(bf16[256,192]{0,1:T(8,128)(2,1)S(1)} %fusion.20), channel_id=2, replica_groups=mesh['exp'=128,'hid'=4] {'hid'}, dimensions={1}, use_global_device_ids=true | all-gather | bytes 491520 | tf_op jit(solution)/shard_map/all_gather | solution.py:85
  202.8 0.7 copy-done.4
  203.6 1.4 convolution_convert_fusion.2
  205.0 2.1 all_to_all.49
  207.0 1.2 convert_multiply_fusion
  208.2 1.4 fusion.25
  209.6 15.9 %all-to-all-start.2 = ((bf16[128,2,1024]{2,1,0:T(2,128)(2,1)}), bf16[128,2,1024]{2,1,0:T(2,128)(2,1)}, u32[]{:S(2)}, u32[]{:S(2)}) async-start(bf16[128,2,1024]{2,1,0:T(2,128)(2,1)} %all_to_all.49), calls=%async_computation.2 | async-start | bytes 1048576 | tf_op jit(solution)/shard_map/all_to_all | solution.py:91
  225.5 1.3 fusion.29
  226.8 0.9 fusion.34
  227.8 1.4 fusion.23
  229.2 1.3 fusion.27
  230.5 1.7 fusion.10
  232.1 1.2 all_to_all.57
  233.4 0.9 gather_fusion.1
  234.3 10.3 %all-to-all-done.2 = bf16[128,2,1024]{2,1,0:T(2,128)(2,1)} async-done(((bf16[128,2,1024]{2,1,0:T(2,128)(2,1)}), bf16[128,2,1024]{2,1,0:T(2,128)(2,1)}, u32[]{:S(2)}, u32[]{:S(2)}) %all-to-all-start.2) | async-done | bytes 524320 | tf_op jit(solution)/shard_map/all_to_all | solution.py:91
  244.6 1.2 all_to_all.51
  245.8 0.9 gather_fusion
  246.7 0.4 fusion.31
  247.1 0.6 pad_maximum_fusion
  (41 shorter events, 0.5 us)
Async XLA Ops:
  7.2 152.0 %copy-start = (bf16[1,192,4096]{2,1,0:T(8,128)(2,1)S(1)}, bf16[1,192,4096]{2,1,0:T(8,128)(2,1)}, u32[]{:S(2)}) copy-start(bf16[1,192,4096]{2,1,0:T(8,128)(2,1)} %param.12) | copy-start | bytes 4718596
  7.2 151.9 %all-gather.7.cloned.1.call-start = ((), (), s32[]{:S(2)}) async-start(), calls=%async_computation.6 | async-start | bytes 2621440 | tf_op jit(solution)/shard_map/all_gather | solution.py:78
  10.3 39.7 %copy-start.5 = (bf16[32,1024]{1,0:T(8,128)(2,1)S(1)}, bf16[32,1024]{1,0:T(8,128)(2,1)}, u32[]{:S(2)}) copy-start(bf16[32,1024]{1,0:T(8,128)(2,1)} %param.8) | copy-start | bytes 196612
  49.1 139.4 %all-gather.5.cloned.1.call-start = ((), (), s32[]{:S(2)}) async-start(), calls=%async_computation.5 | async-start | bytes 2621440 | tf_op jit(solution)/shard_map/all_gather | solution.py:78
  118.1 4.2 %copy-start.10 = (f32[32,8]{0,1:T(8,128)S(1)}, f32[32,8]{0,1:T(8,128)}, u32[]{:S(2)}) copy-start(f32[32,8]{0,1:T(8,128)} %param.10) | copy-start | bytes 3076
  118.1 5.8 %copy-start.11 = (s32[1,768]{1,0:T(1,128)S(1)}, s32[1,768]{1,0:T(1,128)}, u32[]{:S(2)}) copy-start(s32[1,768]{1,0:T(1,128)} %param.11) | copy-start | bytes 9220
  118.1 22.8 %all-to-all-start.1 = ((bf16[4,2,98304]{2,1,0:T(2,128)(2,1)}), bf16[4,2,98304]{2,1,0:T(2,128)(2,1)S(1)}, u32[]{:S(2)}, u32[]{:S(2)}) async-start(bf16[4,2,98304]{2,1,0:T(2,128)(2,1)} %reshape.170), calls=%async_computation.1 | async-start | bytes 3145728 | tf_op jit(solution)/shard_map/all_to_all | solution.py:62
  159.1 2.6 %copy-start.1 = (bf16[256,4096]{1,0:T(8,128)(2,1)S(1)}, bf16[256,4096]{1,0:T(8,128)(2,1)}, u32[]{:S(2)}) copy-start(bf16[256,4096]{1,0:T(8,128)(2,1)} %all-gather.7.cloned.1.call-done) | copy-start | bytes 6291460
  159.1 2.7 %copy-start.12 = (bf16[1,192,4096]{2,1,0:T(8,128)(2,1)S(1)}, bf16[1,192,4096]{2,1,0:T(8,128)(2,1)}, u32[]{:S(2)}) copy-start(bf16[1,192,4096]{2,1,0:T(8,128)(2,1)} %param.13) | copy-start | bytes 4718596
  161.8 10.5 %copy-start.3 = (bf16[1,4,192,1024]{3,2,1,0:T(8,128)(2,1)S(1)}, bf16[1,4,192,1024]{3,2,1,0:T(8,128)(2,1)}, u32[]{:S(2)}) copy-start(bf16[1,4,192,1024]{3,2,1,0:T(8,128)(2,1)} %copy.42) | copy-start | bytes 4718596
  175.7 33.9 %all-to-all-start.4 = ((bf16[128,2,1024]{2,1,0:T(2,128)(2,1)}), bf16[128,2,1024]{2,1,0:T(2,128)(2,1)}, u32[]{:S(2)}, u32[]{:S(2)}) async-start(bf16[128,2,1024]{2,1,0:T(2,128)(2,1)} %all_to_all.55), calls=%async_computation.4 | async-start | bytes 1048576 | tf_op jit(solution)/shard_map/all_to_all | solution.py:91
  188.5 2.6 %copy-start.2 = (bf16[256,4096]{1,0:T(8,128)(2,1)S(1)}, bf16[256,4096]{1,0:T(8,128)(2,1)}, u32[]{:S(2)}) copy-start(bf16[256,4096]{1,0:T(8,128)(2,1)} %all-gather.5.cloned.1.call-done) | copy-start | bytes 6291460
  188.5 2.7 %copy-start.13 = (bf16[1,192,4096]{2,1,0:T(8,128)(2,1)S(1)}, bf16[1,192,4096]{2,1,0:T(8,128)(2,1)}, u32[]{:S(2)}) copy-start(bf16[1,192,4096]{2,1,0:T(8,128)(2,1)} %param.13) | copy-start | bytes 4718596
  202.8 0.7 copy-start.4
  204.9 3.3 %copy-start.7 = (f32[12,12,1]{1,0,2:T(8,128)S(1)}, f32[12,12,1]{1,0,2:T(8,128)}, u32[]{:S(2)}) copy-start(f32[12,12,1]{1,0,2:T(8,128)} %constant.69) | copy-start | bytes 1732
  209.6 35.0 %all-to-all-start.2 = ((bf16[128,2,1024]{2,1,0:T(2,128)(2,1)}), bf16[128,2,1024]{2,1,0:T(2,128)(2,1)}, u32[]{:S(2)}, u32[]{:S(2)}) async-start(bf16[128,2,1024]{2,1,0:T(2,128)(2,1)} %all_to_all.49), calls=%async_computation.2 | async-start | bytes 1048576 | tf_op jit(solution)/shard_map/all_to_all | solution.py:91
  234.2 12.4 %copy-start.8 = (f32[16,8]{1,0:T(8,128)S(1)}, f32[16,8]{1,0:T(8,128)}, u32[]{:S(2)}) copy-start(f32[16,8]{1,0:T(8,128)} %copy.43) | copy-start | bytes 1540
  234.3 12.4 %copy-start.9 = (f32[16,8]{1,0:T(8,128)S(1)}, f32[16,8]{1,0:T(8,128)}, u32[]{:S(2)}) copy-start(f32[16,8]{1,0:T(8,128)} %copy.38) | copy-start | bytes 1540
  245.8 1.3 copy-start.6
Sparse Core Ops, SparseCore 0:
  49.2 29.5 all-gather.6
  80.8 36.1 all-gather.4
where the time goes:
time: 256 us; the launch traced here: 255 us
  blocking collectives  84.4 us (33%)
  local copies, waits for them, and re-layouts  48.2 us (19%)
  starting transfers between devices  32.8 us (13%)
  other arithmetic  29 us (11%)
  waiting for transfers between devices  26.7 us (10%)
  matrix products  19.1 us (7%)
  between operations  14.4 us (6%)
    all_to_all x2, blocking collectives, local(): lax.all_to_all(sending, 'exp', split_axis=0, concat_axis=0, tiled=True)  63.9 us
    all_to_all x2, starting transfers between devices, local(): lax.all_to_all(outgoing, 'exp', split_axis=0, concat_axis=0, tiled=True)  28.6 us
    unnamed x1, other arithmetic  25 us
    unnamed x34, local copies, waits for them, and re-layouts  20.6 us
    all_gather x2, blocking collectives, local(): full_hidden = lax.all_gather(hidden, 'hid', axis=2, tiled=True)  20.5 us
    all_to_all x1, waiting for transfers between devices, local(): lax.all_to_all(w_down, 'hid', split_axis=2, concat_axis=1, tiled=True)  16.4 us
    all_to_all x3, local copies, waits for them, and re-layouts, local(): lax.all_to_all(w_down, 'hid', split_axis=2, concat_axis=1, tiled=True)  14.1 us
    all_to_all x2, waiting for transfers between devices, local(): lax.all_to_all(outgoing, 'exp', split_axis=0, concat_axis=0, tiled=True)  10.3 us
  transfers between devices with their start and end apart: 5, of which 2 were waited for; matrix products, arithmetic and copies ran while one was open for 31% of the time, Pallas kernels for 0%

commit v1 on v0

--- a/solution.py
+++ b/solution.py
@@ -82,7 +82,26 @@
         gate_act = jnp.einsum("esd,efd->esf", expert_in, w_gate, preferred_element_type=jnp.float32)
         up_act = jnp.einsum("esd,efd->esf", expert_in, w_up, preferred_element_type=jnp.float32)
         hidden = (jax.nn.silu(gate_act) * up_act).astype(jnp.bfloat16)
-        full_hidden = lax.all_gather(hidden, "hid", axis=2, tiled=True)
+        item_now = lax.axis_size("hid")
+        met_up = lax.axis_index("hid")
+        k_now, all_values, t_next = (item_now, met_up, hidden.shape[2])
+        pool = tuple((j0 * k_now if ii == 2 else j0 for ii, j0 in enumerate(hidden.shape)))
+        val = jnp.zeros(pool, hidden.dtype)
+        full_hidden = lax.dynamic_update_slice_in_dim(val, hidden, all_values * t_next, axis=2)
+        carry_in = s_next = hidden
+        for j in [*range(1, k_now // 2 + 1)]:
+            carry_in = lax.ppermute(
+                carry_in, "hid", tuple(((ii, (ii + 1) % k_now) for ii in range(k_now)))
+            )
+            full_hidden = lax.dynamic_update_slice_in_dim(
+                full_hidden, carry_in, (all_values - j) % k_now * t_next, axis=2
+            )
+            if 2 * j < k_now:
+                carry = tuple(((ii, (ii - 1) % k_now) for ii in range(k_now)))
+                s_next = lax.ppermute(s_next, "hid", carry)
+                full_hidden = lax.dynamic_update_slice_in_dim(
+                    full_hidden, s_next, (all_values + j) % k_now * t_next, axis=2
+                )
         summed = jnp.einsum(
             "esf,efd->esd", full_hidden, down_cols, preferred_element_type=jnp.float32
         ).astype(jnp.bfloat16)

time: 256 us -> 246 us (0.961)
  blocking collectives: 84.4 us -> 63.9 us
  starting transfers between devices: 32.8 us -> 41.6 us
  waiting for transfers between devices: 26.7 us -> 21.9 us
  local copies, waits for them, and re-layouts: 48.2 us -> 51.6 us
    all_gather x2 -> x0, blocking collectives: 20.5 us -> none  [local(): full_hidden = lax.all_gather(hidden, 'hid', axis=2, tiled=True)]
    ppermute x0 -> x6, starting transfers between devices: none -> 17.2 us  [the longest x4 11.9 us: local(): lax.ppermute(carry_in, 'hid', tuple(((ii, (ii + 1) % k_now) for ii in ran...]
    all_to_all x1, waiting for transfers between devices: 16.4 us -> 0.01 us  [local(): lax.all_to_all(w_down, 'hid', split_axis=2, concat_axis=1, tiled=True)]
    all_to_all x2, waiting for transfers between devices: 10.3 us -> 21.8 us  [local(): lax.all_to_all(outgoing, 'exp', split_axis=0, concat_axis=0, tiled=True)]
    all_to_all x2, starting transfers between devices: 28.6 us -> 20.2 us  [local(): lax.all_to_all(outgoing, 'exp', split_axis=0, concat_axis=0, tiled=True)]
    dynamic_update_slice x0 -> x6, local copies, waits for them, and re-layouts: none -> 3.65 us  [the longest x4 2.73 us: local(): lax.dynamic_update_slice_in_dim(full_hidden, carry_in, (all_values - j) %...]
    unnamed x34 -> x36, local copies, waits for them, and re-layouts: 20.6 us -> 21.2 us
  transfers between devices with their start and end apart: 5 -> 11, of which waited for: 2 -> 2; matrix products, arithmetic and copies ran while one was open for 31% -> 34% of each run, Pallas kernels for 0% -> 0%
where the time goes in v1:
time: 246 us; the launch traced here: 244 us
  blocking collectives  63.9 us (26%)
  local copies, waits for them, and re-layouts  51.6 us (21%)
  starting transfers between devices  41.6 us (17%)
  other arithmetic  29 us (12%)
  waiting for transfers between devices  21.9 us (9%)
  matrix products  21.3 us (9%)
  between operations  14.6 us (6%)
    all_to_all x2, blocking collectives, local(): lax.all_to_all(sending, 'exp', split_axis=0, concat_axis=0, tiled=True)  63.9 us
    unnamed x1, other arithmetic  25 us
    all_to_all x2, waiting for transfers between devices, local(): lax.all_to_all(outgoing, 'exp', split_axis=0, concat_axis=0, tiled=True)  21.8 us
    unnamed x36, local copies, waits for them, and re-layouts  21.2 us
    all_to_all x2, starting transfers between devices, local(): lax.all_to_all(outgoing, 'exp', split_axis=0, concat_axis=0, tiled=True)  20.2 us
    all_to_all x3, local copies, waits for them, and re-layouts, local(): lax.all_to_all(w_down, 'hid', split_axis=2, concat_axis=1, tiled=True)  13 us
    ppermute x4, starting transfers between devices, local(): lax.ppermute(carry_in, 'hid', tuple(((ii, (ii + 1) % k_now) for ii in ran...  11.9 us
    all_to_all x4, local copies, waits for them, and re-layouts, local(): lax.all_to_all(outgoing, 'exp', split_axis=0, concat_axis=0, tiled=True)  6.7 us
  transfers between devices with their start and end apart: 11, of which 2 were waited for; matrix products, arithmetic and copies ran while one was open for 34% of the time, Pallas kernels for 0%

profile of v1, /device:TPU:1, one launch (start us, length us, event | category | flops | bytes accessed | tf_op | source)
XLA Modules:
  0.0 243.8 jit_solution(7714025327580954134)
XLA Ops:
  7.2 0.9 fusion.90
  8.4 0.2 reduce_window_sum.18
  8.5 0.2 select_reduce_fusion
  8.8 0.1 fusion.47
  9.0 1.1 convolution_convert_fusion.1
  10.1 0.2 all_to_all.52
  10.3 37.8 %all_to_all.63 = bf16[128,2,1024]{2,1,0:T(2,128)(2,1)S(1)} all-to-all(bf16[128,2,1024]{2,1,0:T(2,128)(2,1)S(1)} %all_to_all.52), channel_id=1, replica_groups=mesh['exp'=128,'hid'=4] {'exp'}, dimensions={0} | all-to-all | bytes 1048576 | tf_op jit(solution)/shard_map/all_to_all | solution.py:77
  48.0 1.0 all_to_all.54
  49.4 0.2 reduce_window_sum.17
  49.5 0.2 select_reduce_fusion.1
  49.8 0.1 fusion.46
  49.9 0.3 convolution_convert_fusion.3
  50.3 0.2 all_to_all.43
  50.5 26.2 %all_to_all.64 = bf16[128,2,1024]{2,1,0:T(2,128)(2,1)S(1)} all-to-all(bf16[128,2,1024]{2,1,0:T(2,128)(2,1)S(1)} %all_to_all.43), channel_id=1, replica_groups=mesh['exp'=128,'hid'=4] {'exp'}, dimensions={0} | all-to-all | bytes 1048576 | tf_op jit(solution)/shard_map/all_to_all | solution.py:77
  76.7 1.0 all_to_all.45
  77.7 9.9 %copy.47 = bf16[1,192,4096]{1,0,2:T(2,128)(2,1)} copy(bf16[1,192,4096]{2,1,0:T(8,128)(2,1)} %param.14) | data formatting | bytes 3145728 | tf_op args[6]
  87.6 0.5 broadcast.89
  88.1 25.0 %reduce.2 = bf16[4096,192]{1,0:T(8,128)(2,1)} reduce(bf16[4096,1,192]{2,1,0:T(2,128)(2,1)} %bitcast.87, bf16[]{:T(256)} %broadcast.89), dimensions={1}, to_apply=%bitcast.69.reduce_sub_computation | reduce | bytes 3145730
  113.1 5.0 %reshape.164 = bf16[4,2,98304]{2,1,0:T(2,128)(2,1)} reshape(bf16[4096,192]{1,0:T(8,128)(2,1)} %reduce.2) | data formatting | bytes 3145728
  118.1 4.1 %all-to-all-start.1 = ((bf16[4,2,98304]{2,1,0:T(2,128)(2,1)}), bf16[4,2,98304]{2,1,0:T(2,128)(2,1)S(1)}, u32[]{:S(2)}, u32[]{:S(2)}) async-start(bf16[4,2,98304]{2,1,0:T(2,128)(2,1)} %reshape.164), calls=%async_computation.1 | async-start | bytes 3145728 | tf_op jit(solution)/shard_map/all_to_all | solution.py:62
  122.4 0.7 copy.50
  123.2 0.7 copy.45
  123.9 0.6 convert_reduce_fusion
  124.5 3.0 %fusion.4 = f32[256,192]{0,1:T(8,128)S(1)} fusion(bf16[256,4096]{1,0:T(8,128)(2,1)} %all-gather.5.cloned.1.call-done, bf16[1,192,4096]{2,1,0:T(8,128)(2,1)} %param.12), kind=kOutput, calls=%fused_computation.6 | convolution fusion | flops 402653184 | bytes 3866624 | tf_op jit(solution)/shard_map/esd,efd->esf/dot_general | solution.py:82
  127.6 1.5 constant_dynamic-update-slice_fusion.3
  129.1 0.8 copy-done.5
  129.8 3.5 %collective-permute-start.3 = (bf16[1,256,192]{1,2,0:T(8,128)(2,1)}, bf16[1,256,192]{1,2,0:T(8,128)(2,1)}, u32[]{:S(2)}, u32[]{:S(2)}) collective-permute-start(bf16[1,256,192]{1,2,0:T(8,128)(2,1)} %get-tuple-element.17), channel_id=1, source_target_pairs={{0,1},{1,2},{2,3},{3,0},{4,5},{5,6},{6,7},{7,4},{8,9},{9,10},{10,1... | collective-permute-start | bytes 294920 | tf_op jit(solution)/shard_map/ppermute | solution.py:93
  133.4 3.0 %fusion.6 = f32[256,192]{0,1:T(8,128)S(1)} fusion(bf16[256,4096]{1,0:T(8,128)(2,1)} %all-gather.3.cloned.1.call-done, bf16[1,192,4096]{2,1,0:T(8,128)(2,1)} %param.12), kind=kOutput, calls=%fused_computation.8 | convolution fusion | flops 402653184 | bytes 3866624 | tf_op jit(solution)/shard_map/esd,efd->esf/dot_general | solution.py:82
  136.5 1.5 constant_dynamic-update-slice_fusion.7
  138.0 3.1 %collective-permute-start = (bf16[1,256,192]{1,2,0:T(8,128)(2,1)}, bf16[1,256,192]{1,2,0:T(8,128)(2,1)}, u32[]{:S(2)}, u32[]{:S(2)}) collective-permute-start(bf16[1,256,192]{1,2,0:T(8,128)(2,1)} %get-tuple-element.15), channel_id=1, source_target_pairs={{0,1},{1,2},{2,3},{3,0},{4,5},{5,6},{6,7},{7,4},{8,9},{9,10},{10,1... | collective-permute-start | bytes 294920 | tf_op jit(solution)/shard_map/ppermute | solution.py:93
  141.1 4.1 %reshape.165 = bf16[4096,1,192]{2,1,0:T(2,128)(2,1)} reshape(bf16[4,2,98304]{2,1,0:T(2,128)(2,1)S(1)} %all-to-all-done.1) | data formatting | bytes 3145728
  145.2 9.7 %copy.48 = bf16[1,192,4096]{2,1,0:T(8,128)(2,1)} copy(bf16[1,192,4096]{1,0,2:T(2,128)(2,1)} %bitcast.88) | data formatting | bytes 3145728 | tf_op jit(solution)/shard_map/all_to_all | solution.py:62
  154.9 2.9 %all_to_all.47 = bf16[1,192,4,1024]{3,2,1,0:T(4,128)(2,1)S(1)} reshape(bf16[1,192,4096]{2,1,0:T(8,128)(2,1)} %copy.48) | data formatting | bytes 3145728 | tf_op jit(solution)/shard_map/all_to_all | solution.py:62
  157.8 0.5 copy.49
  158.3 3.4 %collective-permute-start.4 = (bf16[1,256,192]{1,2,0:T(8,128)(2,1)}, bf16[1,256,192]{1,2,0:T(8,128)(2,1)S(1)}, u32[]{:S(2)}, u32[]{:S(2)}) collective-permute-start(bf16[1,256,192]{1,2,0:T(8,128)(2,1)} %get-tuple-element.17), channel_id=1, source_target_pairs={{0,3},{1,0},{2,1},{3,2},{4,7},{5,4},{6,5},{7,6},{8,11},{9,8},{10,9... | collective-permute-start | bytes 294920 | tf_op jit(solution)/shard_map/ppermute | solution.py:101
  161.7 1.9 collective-permute-start.1
  163.6 3.4 %collective-permute-start.5 = (bf16[1,256,192]{1,2,0:T(8,128)(2,1)}, bf16[1,256,192]{1,2,0:T(8,128)(2,1)S(1)}, u32[]{:S(2)}, u32[]{:S(2)}) collective-permute-start(bf16[1,256,192]{1,2,0:T(8,128)(2,1)} %collective-permute-done.3), channel_id=1, source_target_pairs={{0,1},{1,2},{2,3},{3,0},{4,5},{5,6},{6,7},{7,4},{8,9},{9,10},{10,1... | collective-permute-start | bytes 294920 | tf_op jit(solution)/shard_map/ppermute | solution.py:93
  167.0 1.9 collective-permute-start.2
  169.0 0.9 constant_dynamic-update-slice_fusion.2
  169.9 0.9 constant_dynamic-update-slice_fusion.6
  170.8 0.7 copy-done.7
  171.6 1.4 convolution_convert_fusion
  173.0 2.2 all_to_all.55
  175.2 12.0 %all-to-all-start.4 = ((bf16[128,2,1024]{2,1,0:T(2,128)(2,1)}), bf16[128,2,1024]{2,1,0:T(2,128)(2,1)}, u32[]{:S(2)}, u32[]{:S(2)}) async-start(bf16[128,2,1024]{2,1,0:T(2,128)(2,1)} %all_to_all.55), calls=%async_computation.4 | async-start | bytes 1048576 | tf_op jit(solution)/shard_map/all_to_all | solution.py:110
  187.2 0.9 constant_dynamic-update-slice_fusion.5
  188.1 0.9 constant_dynamic-update-slice_fusion.4
  189.1 1.4 convolution_convert_fusion.2
  190.5 2.1 all_to_all.49
  192.5 1.2 convert_multiply_fusion
  193.7 1.4 fusion.31
  195.1 11.3 %all-to-all-done.4 = bf16[128,2,1024]{2,1,0:T(2,128)(2,1)} async-done(((bf16[128,2,1024]{2,1,0:T(2,128)(2,1)}), bf16[128,2,1024]{2,1,0:T(2,128)(2,1)}, u32[]{:S(2)}, u32[]{:S(2)}) %all-to-all-start.4) | async-done | bytes 524320 | tf_op jit(solution)/shard_map/all_to_all | solution.py:110
  206.4 8.1 %all-to-all-start.2 = ((bf16[128,2,1024]{2,1,0:T(2,128)(2,1)}), bf16[128,2,1024]{2,1,0:T(2,128)(2,1)}, u32[]{:S(2)}, u32[]{:S(2)}) async-start(bf16[128,2,1024]{2,1,0:T(2,128)(2,1)} %all_to_all.49), calls=%async_computation.2 | async-start | bytes 1048576 | tf_op jit(solution)/shard_map/all_to_all | solution.py:110
  214.6 1.3 fusion.35
  215.9 0.9 fusion.42
  216.9 1.4 fusion.29
  218.2 1.3 fusion.33
  219.6 1.7 fusion.10
  221.2 1.2 all_to_all.57
  222.5 0.9 gather_fusion.1
  223.3 10.5 %all-to-all-done.2 = bf16[128,2,1024]{2,1,0:T(2,128)(2,1)} async-done(((bf16[128,2,1024]{2,1,0:T(2,128)(2,1)}), bf16[128,2,1024]{2,1,0:T(2,128)(2,1)}, u32[]{:S(2)}, u32[]{:S(2)}) %all-to-all-start.2) | async-done | bytes 524320 | tf_op jit(solution)/shard_map/all_to_all | solution.py:110
  233.8 1.2 all_to_all.51
  235.1 0.9 gather_fusion
  235.9 0.4 fusion.37
  236.3 0.6 pad_maximum_fusion
  (61 shorter events, 1.3 us)
Async XLA Ops:
  7.2 120.4 %copy-start = (bf16[1,192,4096]{2,1,0:T(8,128)(2,1)S(1)}, bf16[1,192,4096]{2,1,0:T(8,128)(2,1)}, u32[]{:S(2)}) copy-start(bf16[1,192,4096]{2,1,0:T(8,128)(2,1)} %param.13) | copy-start | bytes 4718596
  7.2 117.3 %all-gather.5.cloned.1.call-start = ((), (), s32[]{:S(2)}) async-start(), calls=%async_computation.6 | async-start | bytes 2621440 | tf_op jit(solution)/shard_map/all_gather | solution.py:78
  10.3 39.7 %copy-start.8 = (bf16[32,1024]{1,0:T(8,128)(2,1)S(1)}, bf16[32,1024]{1,0:T(8,128)(2,1)}, u32[]{:S(2)}) copy-start(bf16[32,1024]{1,0:T(8,128)(2,1)} %param.8) | copy-start | bytes 196612
  49.1 84.3 %all-gather.3.cloned.1.call-start = ((), (), s32[]{:S(2)}) async-start(), calls=%async_computation.5 | async-start | bytes 2621440 | tf_op jit(solution)/shard_map/all_gather | solution.py:78
  118.1 4.2 %copy-start.13 = (f32[32,8]{0,1:T(8,128)S(1)}, f32[32,8]{0,1:T(8,128)}, u32[]{:S(2)}) copy-start(f32[32,8]{0,1:T(8,128)} %param.10) | copy-start | bytes 3076
  118.1 5.8 %copy-start.14 = (s32[1,768]{1,0:T(1,128)S(1)}, s32[1,768]{1,0:T(1,128)}, u32[]{:S(2)}) copy-start(s32[1,768]{1,0:T(1,128)} %param.11) | copy-start | bytes 9220
  118.1 23.0 %all-to-all-start.1 = ((bf16[4,2,98304]{2,1,0:T(2,128)(2,1)}), bf16[4,2,98304]{2,1,0:T(2,128)(2,1)S(1)}, u32[]{:S(2)}, u32[]{:S(2)}) async-start(bf16[4,2,98304]{2,1,0:T(2,128)(2,1)} %reshape.164), calls=%async_computation.1 | async-start | bytes 3145728 | tf_op jit(solution)/shard_map/all_to_all | solution.py:62
  124.5 3.1 %copy-start.1 = (bf16[256,4096]{1,0:T(8,128)(2,1)S(1)}, bf16[256,4096]{1,0:T(8,128)(2,1)}, u32[]{:S(2)}) copy-start(bf16[256,4096]{1,0:T(8,128)(2,1)} %all-gather.5.cloned.1.call-done) | copy-start | bytes 6291460
  129.1 0.8 copy-start.5
  129.8 33.8 %collective-permute-start.3 = (bf16[1,256,192]{1,2,0:T(8,128)(2,1)}, bf16[1,256,192]{1,2,0:T(8,128)(2,1)}, u32[]{:S(2)}, u32[]{:S(2)}) collective-permute-start(bf16[1,256,192]{1,2,0:T(8,128)(2,1)} %get-tuple-element.17), channel_id=1, source_target_pairs={{0,1},{1,2},{2,3},{3,0},{4,5},{5,6},{6,7},{7,4},{8,9},{9,10},{10,1... | collective-permute-start | bytes 294920 | tf_op jit(solution)/shard_map/ppermute | solution.py:93
  133.4 3.1 %copy-start.2 = (bf16[256,4096]{1,0:T(8,128)(2,1)S(1)}, bf16[256,4096]{1,0:T(8,128)(2,1)}, u32[]{:S(2)}) copy-start(bf16[256,4096]{1,0:T(8,128)(2,1)} %all-gather.3.cloned.1.call-done) | copy-start | bytes 6291460
  138.0 29.0 %collective-permute-start = (bf16[1,256,192]{1,2,0:T(8,128)(2,1)}, bf16[1,256,192]{1,2,0:T(8,128)(2,1)}, u32[]{:S(2)}, u32[]{:S(2)}) collective-permute-start(bf16[1,256,192]{1,2,0:T(8,128)(2,1)} %get-tuple-element.15), channel_id=1, source_target_pairs={{0,1},{1,2},{2,3},{3,0},{4,5},{5,6},{6,7},{7,4},{8,9},{9,10},{10,1... | collective-permute-start | bytes 294920 | tf_op jit(solution)/shard_map/ppermute | solution.py:93
  157.8 11.2 %copy-start.6 = (bf16[1,256,768]{1,2,0:T(8,128)(2,1)S(1)}, bf16[1,256,768]{1,2,0:T(8,128)(2,1)}, u32[]{:S(2)}) copy-start(bf16[1,256,768]{1,2,0:T(8,128)(2,1)} %copy-done.5) | copy-start | bytes 1179652
  158.3 12.6 %copy-start.3 = (bf16[1,4,192,1024]{3,2,1,0:T(8,128)(2,1)}, bf16[1,4,192,1024]{3,2,1,0:T(8,128)(2,1)S(1)}, u32[]{:S(2)}) copy-start(bf16[1,4,192,1024]{3,2,1,0:T(8,128)(2,1)S(1)} %copy.49) | copy-start | bytes 4718596
  158.3 12.5 %collective-permute-start.4 = (bf16[1,256,192]{1,2,0:T(8,128)(2,1)}, bf16[1,256,192]{1,2,0:T(8,128)(2,1)S(1)}, u32[]{:S(2)}, u32[]{:S(2)}) collective-permute-start(bf16[1,256,192]{1,2,0:T(8,128)(2,1)} %get-tuple-element.17), channel_id=1, source_target_pairs={{0,3},{1,0},{2,1},{3,2},{4,7},{5,4},{6,5},{7,6},{8,11},{9,8},{10,9... | collective-permute-start | bytes 294920 | tf_op jit(solution)/shard_map/ppermute | solution.py:101
  161.7 25.5 %collective-permute-start.1 = (bf16[1,256,192]{1,2,0:T(8,128)(2,1)}, bf16[1,256,192]{1,2,0:T(8,128)(2,1)}, u32[]{:S(2)}, u32[]{:S(2)}) collective-permute-start(bf16[1,256,192]{1,2,0:T(8,128)(2,1)} %get-tuple-element.15), channel_id=1, source_target_pairs={{0,3},{1,0},{2,1},{3,2},{4,7},{5,4},{6,5},{7,6},{8,11},{9,8},{10,9... | collective-permute-start | bytes 294920 | tf_op jit(solution)/shard_map/ppermute | solution.py:101
  163.6 7.2 %collective-permute-start.5 = (bf16[1,256,192]{1,2,0:T(8,128)(2,1)}, bf16[1,256,192]{1,2,0:T(8,128)(2,1)S(1)}, u32[]{:S(2)}, u32[]{:S(2)}) collective-permute-start(bf16[1,256,192]{1,2,0:T(8,128)(2,1)} %collective-permute-done.3), channel_id=1, source_target_pairs={{0,1},{1,2},{2,3},{3,0},{4,5},{5,6},{6,7},{7,4},{8,9},{9,10},{10,1... | collective-permute-start | bytes 294920 | tf_op jit(solution)/shard_map/ppermute | solution.py:93
  167.0 21.1 %collective-permute-start.2 = (bf16[1,256,192]{1,2,0:T(8,128)(2,1)}, bf16[1,256,192]{1,2,0:T(8,128)(2,1)}, u32[]{:S(2)}, u32[]{:S(2)}) collective-permute-start(bf16[1,256,192]{1,2,0:T(8,128)(2,1)} %collective-permute-done), channel_id=1, source_target_pairs={{0,1},{1,2},{2,3},{3,0},{4,5},{5,6},{6,7},{7,4},{8,9},{9,10},{10,1... | collective-permute-start | bytes 294920 | tf_op jit(solution)/shard_map/ppermute | solution.py:93
  170.8 0.8 copy-start.7
  173.0 16.1 %copy-start.4 = (bf16[1,4,192,1024]{3,2,1,0:T(8,128)(2,1)S(1)}, bf16[1,4,192,1024]{3,2,1,0:T(8,128)(2,1)}, u32[]{:S(2)}) copy-start(bf16[1,4,192,1024]{3,2,1,0:T(8,128)(2,1)} %copy-done.3) | copy-start | bytes 4718596
  175.2 31.3 %all-to-all-start.4 = ((bf16[128,2,1024]{2,1,0:T(2,128)(2,1)}), bf16[128,2,1024]{2,1,0:T(2,128)(2,1)}, u32[]{:S(2)}, u32[]{:S(2)}) async-start(bf16[128,2,1024]{2,1,0:T(2,128)(2,1)} %all_to_all.55), calls=%async_computation.4 | async-start | bytes 1048576 | tf_op jit(solution)/shard_map/all_to_all | solution.py:110
  190.5 3.2 %copy-start.10 = (f32[12,12,1]{1,0,2:T(8,128)S(1)}, f32[12,12,1]{1,0,2:T(8,128)}, u32[]{:S(2)}) copy-start(f32[12,12,1]{1,0,2:T(8,128)} %constant.99) | copy-start | bytes 1732
  206.4 27.4 %all-to-all-start.2 = ((bf16[128,2,1024]{2,1,0:T(2,128)(2,1)}), bf16[128,2,1024]{2,1,0:T(2,128)(2,1)}, u32[]{:S(2)}, u32[]{:S(2)}) async-start(bf16[128,2,1024]{2,1,0:T(2,128)(2,1)} %all_to_all.49), calls=%async_computation.2 | async-start | bytes 1048576 | tf_op jit(solution)/shard_map/all_to_all | solution.py:110
  223.3 12.6 %copy-start.11 = (f32[16,8]{1,0:T(8,128)S(1)}, f32[16,8]{1,0:T(8,128)}, u32[]{:S(2)}) copy-start(f32[16,8]{1,0:T(8,128)} %copy.50) | copy-start | bytes 1540
  223.3 12.6 %copy-start.12 = (f32[16,8]{1,0:T(8,128)S(1)}, f32[16,8]{1,0:T(8,128)}, u32[]{:S(2)}) copy-start(f32[16,8]{1,0:T(8,128)} %copy.45) | copy-start | bytes 1540
  235.0 1.3 copy-start.9
Sparse Core Ops, SparseCore 0:
  49.2 29.5 all-gather.4
  80.8 36.1 all-gather.2
